TPU v7x, 32 devices: a whole 2x2x4 slice. The times are simulated.
32 devices in a mesh: ctx: 16 (over z, x, core), fsdp: 2 (over y).
Axes of the slice: x: 2, y: 2, z: 4, core: 2. Of those that a mesh axis runs over, the one named last changes fastest.
Arguments:
- activations: bfloat16 [4096, 8192], P('ctx', 'fsdp'), may hold values from -8.5 to 8.5
- w_query: bfloat16 [8192, 8192], P('ctx', 'fsdp'), may hold values from -0.044194174 to 0.044194174
- w_key: bfloat16 [8192, 1024], P('ctx', 'fsdp'), may hold values from -0.044194174 to 0.044194174
- w_value: bfloat16 [8192, 1024], P('ctx', 'fsdp'), may hold values from -0.0625 to 0.0625
- seed_words: int32 [1], replicated, may hold values from 0 to 1073741823
- stream_offset: int32 [1], replicated, may hold values from 0 to 1048575
- layer_index: int32 [1], replicated, may hold values from 0 to 79
Outputs:
- attention: bfloat16 [4096, 8192], P('ctx', 'fsdp')
All inputs are finite; a program needn't handle non-finite values.
Results may differ from a plain program's by a relative error of at most 0.007.
Values may be sent and summed in bfloat16 or wider, within the bound.
No kernel may reach another device: no remote copies, remote signals or barrier semaphores. Data moves between devices by JAX's collectives and lax.ppermute only.
A program may use at most 320 MiB of HBM per device.

v0:
```python
import jax
import jax.numpy as jnp
import numpy as np
from jax import lax
from jax.sharding import Mesh
from jax.sharding import PartitionSpec as P

HQ = 64
KV = 8
HD = 128
golden = -1640531535
drop_rate = 0.1
drop_level = 1677722
rope_theta = 500000.0
masked_score = -1e30


def shift_down(values, amount):
    return lax.shift_right_logical(values, jnp.full(values.shape, amount, jnp.int32))


def scramble(values):
    values = jnp.bitwise_xor(values, shift_down(values, 16))
    values = values * jnp.int32(-2048144789)
    values = jnp.bitwise_xor(values, shift_down(values, 13))
    values = values * jnp.int32(-1028477387)
    return jnp.bitwise_xor(values, shift_down(values, 16))


def head_word(seed_words, stream_offset, layer_index, head_ids):
    inner = scramble(head_ids + stream_offset[0])
    middle = scramble(layer_index[0] * jnp.int32(golden) + inner)
    return scramble(seed_words[0] + middle)


def rotation(positions):
    half_width = HD // 2
    exponent = jnp.arange(half_width, dtype=jnp.float32) * 2.0 / HD
    frequency = rope_theta ** (-exponent)
    angles = positions.astype(jnp.float32)[:, None] * frequency[None, :]
    return (jnp.cos(angles), jnp.sin(angles))


def rotate(values, cosine, sine_part):
    half_width = HD // 2
    first_half = values[..., :half_width]
    second_half = values[..., half_width:]
    return jnp.concatenate(
        [
            first_half * cosine - second_half * sine_part,
            second_half * cosine + first_half * sine_part,
        ],
        axis=-1,
    )


def attend(queries, keys, values, query_pos, words, spans):
    score_scale = HD ** (-0.5)
    pieces = []
    for first, count, span in spans:
        block_pos = query_pos[first : first + count]
        key_pos = jnp.arange(span, dtype=jnp.int32)
        scores = (
            jnp.einsum(
                "qhe,ke->hqk",
                queries[first : first + count],
                keys[:span],
                preferred_element_type=jnp.float32,
            )
            * score_scale
        )
        visible = key_pos[None, None, :] <= block_pos[None, :, None]
        highest = jnp.max(jnp.where(visible, scores, masked_score), axis=2, keepdims=True)
        weights = jnp.where(visible, jnp.exp(scores - highest), 0.0)
        summed = jnp.sum(weights, axis=2)
        row_words = scramble(jnp.bitwise_xor(words[:, None], block_pos[None, :]))
        mixed_bits = scramble(row_words[:, :, None] + (key_pos * jnp.int32(golden))[None, None, :])
        keep = shift_down(mixed_bits, 8) >= drop_level
        dropped = jnp.where(keep, weights, 0.0).astype(jnp.bfloat16)
        attended = jnp.einsum(
            "hqk,ke->qhe", dropped, values[:span], preferred_element_type=jnp.float32
        )
        pieces.append((attended / (summed * (1.0 - drop_rate)).T[:, :, None]).astype(jnp.bfloat16))
    return jnp.concatenate(pieces, axis=0)


def shards(activations, w_query, w_key, w_value, seed_words, stream_offset, layer_index):
    n_t = lax.axis_size("ct")
    n_g = lax.axis_size("cg")
    t = lax.axis_index("ct")
    g = lax.axis_index("cg")
    f = lax.axis_index("fsdp")
    tok = activations.shape[0]
    d_rows = w_query.shape[0]
    group_heads = HQ // KV
    local_heads = w_query.shape[1] // HD
    qcols = group_heads * HD
    width = qcols + 2 * HD
    rows = n_g * tok
    length = n_t * rows
    half_rows = lax.all_gather(activations, "cg", axis=0, tiled=True)
    grp_rows = lax.all_gather(half_rows, "fsdp", axis=1, tiled=True)
    local_w = jnp.concatenate(
        [
            w_query.reshape(d_rows, n_g, qcols),
            w_key.reshape(d_rows, n_g, HD),
            w_value.reshape(d_rows, n_g, HD),
        ],
        axis=2,
    )
    received = [lax.dynamic_index_in_dim(local_w, g, 1, keepdims=False)]
    for shift in range(1, n_g):
        outgoing = lax.dynamic_index_in_dim(local_w, (g + shift) % n_g, 1, keepdims=False)
        perm = [(i, (i + shift) % n_g) for i in range(n_g)]
        received.append(lax.ppermute(outgoing, "cg", perm))
    by_shift = jnp.stack(received, axis=0)
    mine = jnp.take(by_shift, (g - jnp.arange(n_g, dtype=jnp.int32)) % n_g, axis=0)
    every = lax.all_gather(mine, "ct", axis=0, tiled=False).reshape(n_t * n_g * d_rows, width)
    mixed = jnp.dot(grp_rows, every, preferred_element_type=jnp.float32)
    positions = t * rows + jnp.arange(rows, dtype=jnp.int32)
    cosine, sine_part = rotation(positions)
    queries = rotate(
        mixed[:, :qcols].reshape(rows, group_heads, HD), cosine[:, None, :], sine_part[:, None, :]
    ).astype(jnp.bfloat16)
    keys = rotate(mixed[:, qcols : qcols + HD], cosine, sine_part).astype(jnp.bfloat16)
    values = mixed[:, qcols + HD :].astype(jnp.bfloat16)
    pair = lax.all_gather(jnp.stack([keys, values], axis=1), "ct", axis=0, tiled=True)
    all_keys = pair[:, 0]
    all_values = pair[:, 1]
    if group_heads % n_t == 0:
        owned = group_heads // n_t
        spread = lax.all_to_all(
            queries.reshape(rows, n_t, owned, HD), "ct", split_axis=1, concat_axis=0, tiled=True
        ).reshape(length, owned, HD)
        head_local = g * group_heads + t * owned + jnp.arange(owned, dtype=jnp.int32)
        words = head_word(seed_words, stream_offset, layer_index, f * local_heads + head_local)
        block = min(length, 512)
        spans = [(i * block, block, (i + 1) * block) for i in range(length // block)]
        out = attend(
            spread, all_keys, all_values, jnp.arange(length, dtype=jnp.int32), words, spans
        )
        out = lax.all_to_all(
            out.reshape(n_t, rows, owned, HD), "ct", split_axis=0, concat_axis=2, tiled=True
        ).reshape(rows, qcols)
    else:
        head_local = g * group_heads + jnp.arange(group_heads, dtype=jnp.int32)
        words = head_word(seed_words, stream_offset, layer_index, f * local_heads + head_local)
        out = attend(queries, all_keys, all_values, positions, words, [(0, rows, length)])
        out = out.reshape(rows, qcols)
    returned = lax.all_to_all(
        out.reshape(n_g, tok, qcols), "cg", split_axis=0, concat_axis=2, tiled=True
    )
    return returned.reshape(tok, n_g * qcols)


def solution(mesh):
    ctx = mesh.shape["ctx"]
    fsdp = mesh.shape["fsdp"]
    n_g = KV // fsdp
    n_t = ctx // n_g
    order = [mesh.axis_names.index("ctx"), mesh.axis_names.index("fsdp")]
    devices = np.transpose(mesh.devices, order).reshape(n_t, n_g, fsdp)
    grid = Mesh(devices, ("ct", "cg", "fsdp"))
    spec = P(("ct", "cg"), "fsdp")
    placed = (spec, spec, spec, spec, P(), P(), P())
    return jax.shard_map(shards, mesh=grid, in_specs=placed, out_specs=spec, check_vma=False)
```

profile of v0, /device:TPU:0, one launch (start us, length us, event | category | flops | bytes accessed | tf_op | source)
XLA Modules:
  0.0 953.2 jit_solution(8433113393694348878)
XLA Ops:
  7.3 62.6 %all-gather.7.cloned.1.call-done = bf16[1024,4096]{1,0:T(8,128)(2,1)} async-done(((bf16[256,4096]{1,0:T(8,128)(2,1)}), bf16[1024,4096]{1,0:T(8,128)(2,1)}) %all-gather.7.cloned.1.call-update) | async-done | bytes 8388624 | tf_op jit(solution)/shard_map/all_gather | solution.py:101
  70.1 6.5 copy.73
  77.1 5.7 pad_maximum_fusion
  93.9 21.6 %collective-permute-done = bf16[512,1280]{1,0:T(8,128)(2,1)} collective-permute-done((bf16[512,1280]{1,0:T(8,128)(2,1)}, bf16[512,1280]{1,0:T(8,128)(2,1)}, u32[]{:S(2)}, u32[]{:S(2)}) %collective-permute-start) | collective-permute-done | bytes 1310752 | tf_op jit(solution)/shard_map/ppermute | solution.py:115
  115.4 6.9 collective-permute-done.1
  122.3 22.3 %collective-permute-done.2 = bf16[512,1280]{1,0:T(8,128)(2,1)} collective-permute-done((bf16[512,1280]{1,0:T(8,128)(2,1)}, bf16[512,1280]{1,0:T(8,128)(2,1)}, u32[]{:S(2)}, u32[]{:S(2)}) %collective-permute-start.2) | collective-permute-done | bytes 1310752 | tf_op jit(solution)/shard_map/ppermute | solution.py:115
  144.7 5.2 pad_maximum_fusion.1
  149.9 5.7 gather_fusion
  155.5 5.3 bitcast_select_fusion.24
  172.5 97.9 %all-gather.9.cloned.1.call-done = bf16[1024,8192]{1,0:T(8,128)(2,1)} async-done(((bf16[1024,4096]{1,0:T(8,128)(2,1)}), bf16[1024,8192]{1,0:T(8,128)(2,1)}) %all-gather.9.cloned.1.call-update) | async-done | bytes 16777232 | tf_op jit(solution)/shard_map/all_gather | solution.py:102
  270.4 358.5 %all-gather.5.cloned.1.call-done = bf16[4,4,512,1280]{3,2,1,0:T(8,128)(2,1)} async-done(((bf16[1,4,512,1280]{3,2,1,0:T(8,128)(2,1)}), bf16[4,4,512,1280]{3,2,1,0:T(8,128)(2,1)}) %all-gather.5.cloned.1.call-update) | async-done | bytes 20971536 | tf_op jit(solution)/shard_map/all_gather | solution.py:118
  628.9 27.5 %convolution_bitcast_fusion = f32[1024,1280]{0,1:T(8,128)S(1)} fusion(bf16[8192,1280]{1,0:T(8,128)(2,1)} %bitcast.392, bf16[1024,8192]{1,0:T(8,128)(2,1)} %all-gather.9.cloned.1.call-done), kind=kOutput, calls=%fused_computation.119 | convolution fusion | flops 21474836480 | bytes 42991616 | tf_op jit(solution)/shard_map/dot_general | solution.py:119
  684.6 65.1 %all-to-all-done = bf16[1024,4,2,128]{3,0,2,1:T(8,128)(2,1)S(1)} async-done(((bf16[1024,4,2,128]{3,0,2,1:T(8,128)(2,1)}), bf16[1024,4,2,128]{3,0,2,1:T(8,128)(2,1)S(1)}, u32[]{:S(2)}, u32[]{:S(2)}) %all-to-all-start) | async-done | bytes 2097184 | tf_op jit(solution)/shard_map/all_to_all | solution.py:132
  751.2 13.2 %fusion.317 = (f32[2,512]{1,0:T(2,128)S(1)}, bf16[2,512,4096]{1,2,0:T(8,128)(2,1)}) fusion(pred[512,4096]{0,1:T(8,128)(4,1)} %iota_compare_fusion, bf16[4096,2,128]{0,2,1:T(8,128)(2,1)} %all-gather.11.cloned.1.call-done, bf16[4096,2,128]{2,0,1:T(8,128)(2,1)} %bitcast.379), kind=kOutput, calls=%fused_computation.439 | convolution fusion | flops 2176847872 | bytes 15208448 | tf_op jit(solution)/shard_map/sub | solution.py:74
  764.4 10.0 %fusion.312 = (f32[2,512]{1,0:T(2,128)S(1)}, bf16[2,512,3584]{1,2,0:T(8,128)(2,1)}) fusion(pred[512,3584]{0,1:T(8,128)(4,1)} %iota_compare_fusion.1, bf16[4096,2,128]{0,2,1:T(8,128)(2,1)} %all-gather.11.cloned.1.call-done, bf16[4096,2,128]{2,0,1:T(8,128)(2,1)S(1)} %bitcast.380), kind=kOutput, calls=%fused_computation.438 | convolution fusion | flops 1904741888 | bytes 13373440 | tf_op jit(solution)/shard_map/sub | solution.py:74
  774.5 10.0 %fusion.307 = (f32[2,512]{1,0:T(2,128)S(1)}, bf16[2,512,3072]{1,2,0:T(8,128)(2,1)}) fusion(pred[512,3072]{0,1:T(8,128)(4,1)} %iota_compare_fusion.2, bf16[4096,2,128]{0,2,1:T(8,128)(2,1)} %all-gather.11.cloned.1.call-done, bf16[4096,2,128]{2,0,1:T(8,128)(2,1)S(1)} %bitcast.381), kind=kOutput, calls=%fused_computation.437 | convolution fusion | flops 1632635904 | bytes 11538432 | tf_op jit(solution)/shard_map/sub | solution.py:74
  784.5 7.2 fusion.302
  791.7 8.3 fusion.297
  825.9 5.0 fusion.131
  831.0 5.6 fusion.140
  836.7 6.6 fusion.149
  843.3 7.2 fusion.146
  855.3 51.1 %all_to_all.45 = bf16[4,1024,2,128]{3,2,1,0:T(2,128)(2,1)S(1)} all-to-all(bf16[4,1024,2,128]{3,2,1,0:T(2,128)(2,1)S(1)} %bitcast.374), channel_id=1, replica_groups=mesh['ct'=4,'cg'=4,'fsdp'=2] {'ct'}, dimensions={0} | all-to-all | bytes 4194304 | tf_op jit(solution)/shard_map/all_to_all | solution.py:142
  910.5 29.3 %all_to_all.46 = bf16[4,256,1024]{2,1,0:T(8,128)(2,1)S(1)} all-to-all(bf16[4,256,1024]{2,1,0:T(8,128)(2,1)} %reshape_reshape.3), channel_id=1, replica_groups=mesh['ct'=4,'cg'=4,'fsdp'=2] {'cg'}, dimensions={0} | all-to-all | bytes 4194304 | tf_op jit(solution)/shard_map/all_to_all | solution.py:150
  (134 shorter events, 92.9 us)
Async XLA Ops:
  6.5 63.4 %all-gather.7.cloned.1.call-start = ((), (), s32[]{:S(2)}) async-start(), calls=%async_computation.4 | async-start | bytes 10485760 | tf_op jit(solution)/shard_map/all_gather | solution.py:101
  7.3 263.1 %all-gather.9.cloned.1.call-start = ((), (), s32[]{:S(2)}) async-start(), calls=%async_computation.5 | async-start | bytes 25165824 | tf_op jit(solution)/shard_map/all_gather | solution.py:102
  70.0 558.9 %all-gather.5.cloned.1.call-start = ((), (), s32[]{:S(2)}) async-start(), calls=%async_computation.3 | async-start | bytes 26214400 | tf_op jit(solution)/shard_map/all_gather | solution.py:118
  70.0 6.6 copy-start.2
  70.1 6.8 copy-start.3
  87.5 27.9 %collective-permute-start = (bf16[512,1280]{1,0:T(8,128)(2,1)}, bf16[512,1280]{1,0:T(8,128)(2,1)}, u32[]{:S(2)}, u32[]{:S(2)}) collective-permute-start(bf16[512,1280]{1,0:T(8,128)(2,1)} %bitcast.389), channel_id=1, source_target_pairs={{0,2},{2,4},{4,6},{6,0},{1,3},{3,5},{5,7},{7,1},{8,10},{10,12},{12... | collective-permute-start | bytes 3932168 | tf_op jit(solution)/shard_map/ppermute | solution.py:115
  90.3 32.0 %collective-permute-start.1 = (bf16[512,1280]{1,0:T(8,128)(2,1)}, bf16[512,1280]{1,0:T(8,128)(2,1)}, u32[]{:S(2)}, u32[]{:S(2)}) collective-permute-start(bf16[512,1280]{1,0:T(8,128)(2,1)} %bitcast.390), channel_id=1, source_target_pairs={{0,4},{2,6},{4,0},{6,2},{1,5},{3,7},{5,1},{7,3},{8,12},{10,14},{12... | collective-permute-start | bytes 3932168 | tf_op jit(solution)/shard_map/ppermute | solution.py:115
  91.9 52.8 %collective-permute-start.2 = (bf16[512,1280]{1,0:T(8,128)(2,1)}, bf16[512,1280]{1,0:T(8,128)(2,1)}, u32[]{:S(2)}, u32[]{:S(2)}) collective-permute-start(bf16[512,1280]{1,0:T(8,128)(2,1)} %bitcast.391), channel_id=1, source_target_pairs={{0,6},{2,0},{4,2},{6,4},{1,7},{3,1},{5,3},{7,5},{8,14},{10,8},{12,... | collective-permute-start | bytes 3932168 | tf_op jit(solution)/shard_map/ppermute | solution.py:115
  160.9 590.3 %all-gather.11.cloned.1.call-start = ((), (), s32[]{:S(2)}) async-start(), calls=%async_computation.6 | async-start | bytes 2621440 | tf_op jit(solution)/shard_map/all_gather | solution.py:127
  672.5 77.3 %all-to-all-start = ((bf16[1024,4,2,128]{3,0,2,1:T(8,128)(2,1)}), bf16[1024,4,2,128]{3,0,2,1:T(8,128)(2,1)S(1)}, u32[]{:S(2)}, u32[]{:S(2)}) async-start(bf16[1024,4,2,128]{3,0,2,1:T(8,128)(2,1)} %pad_maximum_fusion.2), calls=%async_computation | async-start | bytes 4194304 | tf_op jit(solution)/shard_map/all_to_all | solution.py:132
  751.2 13.2 %copy-start = (bf16[4,1024,1,2,128]{4,1,0,3,2:T(8,128)(2,1)S(1)}, bf16[4,1024,1,2,128]{4,1,0,3,2:T(8,128)(2,1)}, u32[]{:S(2)}) copy-start(bf16[4,1024,1,2,128]{4,1,0,3,2:T(8,128)(2,1)} %copy.82) | copy-start | bytes 6291460
  807.0 6.0 copy-start.5
  818.4 7.4 slice-start
  821.8 9.2 slice-start.2
  825.9 5.1 copy-start.9
  825.9 5.1 copy-start.13
  825.9 10.7 %slice-start.4 = ((s8[7340032]{0:T(1024)(128)(4,1)}), s8[4194304]{0:T(1024)(128)(4,1)S(1)}, s32[]{:S(2)}) async-start(s8[7340032]{0:T(1024)(128)(4,1)} %bitcast.397), calls=%async_computation.11 | async-start | bytes 8388608
  830.9 5.7 copy-start.8
  830.9 5.7 copy-start.12
  831.0 5.7 slice-start.5
  831.0 12.3 %slice-start.6 = ((s8[8388608]{0:T(1024)(128)(4,1)}), s8[4194304]{0:T(1024)(128)(4,1)S(1)}, s32[]{:S(2)}) async-start(s8[8388608]{0:T(1024)(128)(4,1)} %bitcast.399), calls=%async_computation.13 | async-start | bytes 8388608
  836.6 6.7 copy-start.7
  836.7 6.7 copy-start.11
  836.7 6.7 slice-start.7
  (10 other events, 34.6 us)
Sparse Core Ops, SparseCore 0:
  8.9 60.9 all-gather.6
  71.5 198.8 all-gather.8
  272.0 356.8 all-gather.4
  660.8 79.2 all-gather.10
where the time goes:
time: 961 us; the launch traced here: 953 us
  waiting for transfers between devices  636 us (66%)
  matrix products  120 us (12%)
  blocking collectives  80.3 us (8%)
  other arithmetic  50.2 us (5%)
  local copies, waits for them, and re-layouts  45.1 us (5%)
  between operations  15.8 us (2%)
    all_gather x1, waiting for transfers between devices, shards(): lax.all_gather(mine, 'ct', axis=0, tiled=False)  358 us
    all_gather x1, waiting for transfers between devices, shards(): grp_rows = lax.all_gather(half_rows, 'fsdp', axis=1, tiled=True)  97.9 us
    all_to_all x1, waiting for transfers between devices, shards(): lax.all_to_all(queries.reshape(rows, n_t, owned, HD), 'ct', split_axis=1,...  65.1 us
    all_gather x1, waiting for transfers between devices, shards(): half_rows = lax.all_gather(activations, 'cg', axis=0, tiled=True)  62.6 us
    sub x6, matrix products, attend(): weights = jnp.where(visible, jnp.exp(scores - highest), 0.0)  53.2 us
    all_to_all x1, blocking collectives, shards(): lax.all_to_all(out.reshape(n_t, rows, owned, HD), 'ct', split_axis=0, con...  51.1 us
    ppermute x3, waiting for transfers between devices, shards(): received.append(lax.ppermute(outgoing, 'cg', perm))  50.8 us
    dot_general x8, matrix products, attend(): jnp.einsum('hqk,ke->qhe', dropped, values[:span], preferred_element_type=...  36.1 us
  transfers between devices with their start and end apart: 8, of which 7 were waited for; matrix products, arithmetic and copies ran while one was open for 7% of the time, Pallas kernels for 0%

commit v1 on v0

--- a/solution.py
+++ b/solution.py
@@ -13,6 +13,18 @@
 drop_level = 1677722
 rope_theta = 500000.0
 masked_score = -1e30
+
+
+def doubled_up(x, axis, dim):
+    ways, here, hop = (lax.axis_size(axis), lax.axis_index(axis), x.shape[dim])
+    line, have = (x, 1)
+    while have < ways:
+        line = jnp.concatenate(
+            [line, lax.ppermute(line, axis, [(d, (d - have) % ways) for d in range(ways)])],
+            axis=dim,
+        )
+        have = 2 * have
+    return jnp.roll(line, here * hop, axis=dim)
 
 
 def shift_down(values, amount):
@@ -99,7 +111,7 @@
     rows = n_g * tok
     length = n_t * rows
     half_rows = lax.all_gather(activations, "cg", axis=0, tiled=True)
-    grp_rows = lax.all_gather(half_rows, "fsdp", axis=1, tiled=True)
+    grp_rows = doubled_up(half_rows, "fsdp", 1)
     local_w = jnp.concatenate(
         [
             w_query.reshape(d_rows, n_g, qcols),

time: 961 us -> 846 us (0.88)
  waiting for transfers between devices: 636 us -> 505 us
  matrix products: 120 us -> 132 us
    all_gather x1, waiting for transfers between devices: 358 us -> 176 us  [shards(): lax.all_gather(mine, 'ct', axis=0, tiled=False)]
    ppermute x0 -> x1, waiting for transfers between devices: none -> 168 us  [doubled_up(): lax.ppermute(line, axis, [(d, (d - have) % ways) for d in range(ways)])]
    all_gather x1 -> x0, waiting for transfers between devices: 97.9 us -> none  [shards(): grp_rows = lax.all_gather(half_rows, 'fsdp', axis=1, tiled=True)]
    all_gather x1, waiting for transfers between devices: 62.6 us -> 0.02 us  [shards(): half_rows = lax.all_gather(activations, 'cg', axis=0, tiled=True)]
    ppermute x3, waiting for transfers between devices: 50.8 us -> 90 us  [shards(): received.append(lax.ppermute(outgoing, 'cg', perm))]
    dot_general x1, matrix products: 27.5 us -> 38.5 us  [shards(): mixed = jnp.dot(grp_rows, every, preferred_element_type=jnp.float32)]
  transfers between devices with their start and end apart: 8 -> 8, of which waited for: 7 -> 6; matrix products, arithmetic and copies ran while one was open for 7% -> 7% of each run, Pallas kernels for 0% -> 0%
where the time goes in v1:
time: 846 us; the launch traced here: 842 us
  waiting for transfers between devices  505 us (60%)
  matrix products  132 us (16%)
  blocking collectives  79.5 us (9%)
  other arithmetic  54.3 us (6%)
  local copies, waits for them, and re-layouts  46.5 us (5%)
  between operations  16 us (2%)
  starting transfers between devices  8.95 us (1%)
    all_gather x1, waiting for transfers between devices, shards(): lax.all_gather(mine, 'ct', axis=0, tiled=False)  176 us
    ppermute x1, waiting for transfers between devices, doubled_up(): lax.ppermute(line, axis, [(d, (d - have) % ways) for d in range(ways)])  168 us
    ppermute x3, waiting for transfers between devices, shards(): received.append(lax.ppermute(outgoing, 'cg', perm))  90 us
    all_to_all x1, waiting for transfers between devices, shards(): lax.all_to_all(queries.reshape(rows, n_t, owned, HD), 'ct', split_axis=1,...  70.1 us
    sub x6, matrix products, attend(): weights = jnp.where(visible, jnp.exp(scores - highest), 0.0)  51.5 us
    all_to_all x1, blocking collectives, shards(): lax.all_to_all(out.reshape(n_t, rows, owned, HD), 'ct', split_axis=0, con...  50.2 us
    dot_general x1, matrix products, shards(): mixed = jnp.dot(grp_rows, every, preferred_element_type=jnp.float32)  38.5 us
    dot_general x8, matrix products, attend(): jnp.einsum('hqk,ke->qhe', dropped, values[:span], preferred_element_type=...  38.2 us
  transfers between devices with their start and end apart: 8, of which 6 were waited for; matrix products, arithmetic and copies ran while one was open for 7% of the time, Pallas kernels for 0%

profile of v1, /device:TPU:0, one launch (start us, length us, event | category | flops | bytes accessed | tf_op | source)
XLA Modules:
  0.0 841.9 jit_solution(1316681520683718311)
XLA Ops:
  9.9 6.5 copy.73
  16.3 5.4 pad_maximum_fusion
  34.5 50.8 %collective-permute-done.3 = bf16[512,1280]{1,0:T(8,128)(2,1)} collective-permute-done((bf16[512,1280]{1,0:T(8,128)(2,1)}, bf16[512,1280]{1,0:T(8,128)(2,1)}, u32[]{:S(2)}, u32[]{:S(2)}) %collective-permute-start.3) | collective-permute-done | bytes 1310752 | tf_op jit(solution)/shard_map/ppermute | solution.py:127
  85.3 38.4 %collective-permute-done.2 = bf16[512,1280]{1,0:T(8,128)(2,1)} collective-permute-done((bf16[512,1280]{1,0:T(8,128)(2,1)}, bf16[512,1280]{1,0:T(8,128)(2,1)}, u32[]{:S(2)}, u32[]{:S(2)}) %collective-permute-start.2) | collective-permute-done | bytes 1310752 | tf_op jit(solution)/shard_map/ppermute | solution.py:127
  124.4 5.2 pad_maximum_fusion.1
  129.7 5.6 gather_fusion
  135.3 5.3 bitcast_select_fusion.24
  153.8 167.6 %collective-permute-done = bf16[1024,4096]{1,0:T(8,128)(2,1)} collective-permute-done((bf16[1024,4096]{1,0:T(8,128)(2,1)}, bf16[1024,4096]{1,0:T(8,128)(2,1)}, u32[]{:S(2)}, u32[]{:S(2)}) %collective-permute-start) | collective-permute-done | bytes 8388640 | tf_op jit(solution)/shard_map/ppermute | solution.py:23
  321.4 176.3 %all-gather.6.cloned.1.call-done = bf16[4,4,512,1280]{3,2,1,0:T(8,128)(2,1)} async-done(((bf16[1,4,512,1280]{3,2,1,0:T(8,128)(2,1)}), bf16[4,4,512,1280]{3,2,1,0:T(8,128)(2,1)}) %all-gather.6.cloned.1.call-update) | async-done | bytes 20971536 | tf_op jit(solution)/shard_map/all_gather | solution.py:130
  497.7 38.5 %fusion.15 = f32[1024,1280]{1,0:T(8,128)} fusion(bf16[8192,1280]{1,0:T(8,128)(2,1)} %bitcast.391, s32[]{:T(128)S(6)} %select_n.173, bf16[1024,4096]{1,0:T(8,128)(2,1)} %all-gather.4.cloned.1.call-done, bf16[1024,4096]{1,0:T(8,128)(2,1)} %collective-permute-done), kind=kOutput, calls=%fused_computation.29 | convolution fusion | flops 21541945344 | bytes 42991620 | tf_op jit(solution)/shard_map/dot_general | solution.py:131
  566.4 70.1 %all-to-all-done = bf16[1024,4,2,128]{3,0,2,1:T(8,128)(2,1)S(1)} async-done(((bf16[1024,4,2,128]{3,0,2,1:T(8,128)(2,1)}), bf16[1024,4,2,128]{3,0,2,1:T(8,128)(2,1)S(1)}, u32[]{:S(2)}, u32[]{:S(2)}) %all-to-all-start) | async-done | bytes 2097184 | tf_op jit(solution)/shard_map/all_to_all | solution.py:144
  649.4 4.9 fusion.303
  654.3 8.0 fusion.304
  662.4 7.3 fusion.309
  669.6 9.3 %fusion.314 = (f32[2,512]{1,0:T(2,128)S(1)}, bf16[2,512,3072]{1,2,0:T(8,128)(2,1)}) fusion(pred[512,3072]{0,1:T(8,128)(4,1)} %iota_compare_fusion.2, bf16[4096,2,128]{2,0,1:T(8,128)(2,1)} %all-gather.8.cloned.1.call-done, bf16[4096,2,128]{2,0,1:T(8,128)(2,1)S(1)} %bitcast.383), kind=kOutput, calls=%fused_computation.447 | convolution fusion | flops 1632635904 | bytes 11538432 | tf_op jit(solution)/shard_map/sub | solution.py:86
  678.9 10.5 %fusion.319 = (f32[2,512]{1,0:T(2,128)S(1)}, bf16[2,512,3584]{1,2,0:T(8,128)(2,1)}) fusion(pred[512,3584]{0,1:T(8,128)(4,1)} %iota_compare_fusion.1, bf16[4096,2,128]{2,0,1:T(8,128)(2,1)} %all-gather.8.cloned.1.call-done, bf16[4096,2,128]{2,0,1:T(8,128)(2,1)S(1)} %bitcast.384), kind=kOutput, calls=%fused_computation.448 | convolution fusion | flops 1904741888 | bytes 13373440 | tf_op jit(solution)/shard_map/sub | solution.py:86
  689.4 11.8 %fusion.324 = (f32[2,512]{1,0:T(2,128)S(1)}, bf16[2,512,4096]{1,2,0:T(8,128)(2,1)}) fusion(pred[512,4096]{0,1:T(8,128)(4,1)} %iota_compare_fusion, bf16[4096,2,128]{2,0,1:T(8,128)(2,1)} %all-gather.8.cloned.1.call-done, bf16[4096,2,128]{2,0,1:T(8,128)(2,1)S(1)} %bitcast.385), kind=kOutput, calls=%fused_computation.449 | convolution fusion | flops 2176847872 | bytes 15208448 | tf_op jit(solution)/shard_map/sub | solution.py:86
  714.4 5.2 fusion.136
  719.7 5.8 fusion.145
  725.5 6.6 fusion.154
  732.2 7.7 fusion.151
  739.9 4.7 copy.127
  744.6 50.2 %all_to_all.45 = bf16[4,1024,2,128]{3,2,1,0:T(2,128)(2,1)S(1)} all-to-all(bf16[4,1024,2,128]{3,2,1,0:T(2,128)(2,1)S(1)} %bitcast.373), channel_id=1, replica_groups=mesh['ct'=4,'cg'=4,'fsdp'=2] {'ct'}, dimensions={0} | all-to-all | bytes 4194304 | tf_op jit(solution)/shard_map/all_to_all | solution.py:154
  798.9 29.3 %all_to_all.46 = bf16[4,256,1024]{2,1,0:T(8,128)(2,1)S(1)} all-to-all(bf16[4,256,1024]{2,1,0:T(8,128)(2,1)} %reshape_reshape.3), channel_id=1, replica_groups=mesh['ct'=4,'cg'=4,'fsdp'=2] {'cg'}, dimensions={0} | all-to-all | bytes 4194304 | tf_op jit(solution)/shard_map/all_to_all | solution.py:162
  (140 shorter events, 94.8 us)
Async XLA Ops:
  6.5 134.1 %all-gather.4.cloned.1.call-start = ((), (), s32[]{:S(2)}) async-start(), calls=%async_computation.3 | async-start | bytes 10485760 | tf_op jit(solution)/shard_map/all_gather | solution.py:113
  7.3 490.4 %all-gather.6.cloned.1.call-start = ((), (), s32[]{:S(2)}) async-start(), calls=%async_computation.4 | async-start | bytes 26214400 | tf_op jit(solution)/shard_map/all_gather | solution.py:130
  26.2 59.1 %collective-permute-start.3 = (bf16[512,1280]{1,0:T(8,128)(2,1)}, bf16[512,1280]{1,0:T(8,128)(2,1)}, u32[]{:S(2)}, u32[]{:S(2)}) collective-permute-start(bf16[512,1280]{1,0:T(8,128)(2,1)} %bitcast.388), channel_id=1, source_target_pairs={{0,6},{2,0},{4,2},{6,4},{1,7},{3,1},{5,3},{7,5},{8,14},{10,8},{12,... | collective-permute-start | bytes 3932168 | tf_op jit(solution)/shard_map/ppermute | solution.py:127
  31.0 92.7 %collective-permute-start.2 = (bf16[512,1280]{1,0:T(8,128)(2,1)}, bf16[512,1280]{1,0:T(8,128)(2,1)}, u32[]{:S(2)}, u32[]{:S(2)}) collective-permute-start(bf16[512,1280]{1,0:T(8,128)(2,1)} %bitcast.389), channel_id=1, source_target_pairs={{0,4},{2,6},{4,0},{6,2},{1,5},{3,7},{5,1},{7,3},{8,12},{10,14},{12... | collective-permute-start | bytes 3932168 | tf_op jit(solution)/shard_map/ppermute | solution.py:127
  33.0 91.4 %collective-permute-start.1 = (bf16[512,1280]{1,0:T(8,128)(2,1)}, bf16[512,1280]{1,0:T(8,128)(2,1)}, u32[]{:S(2)}, u32[]{:S(2)}) collective-permute-start(bf16[512,1280]{1,0:T(8,128)(2,1)} %bitcast.390), channel_id=1, source_target_pairs={{0,2},{2,4},{4,6},{6,0},{1,3},{3,5},{5,7},{7,1},{8,10},{10,12},{12... | collective-permute-start | bytes 3932168 | tf_op jit(solution)/shard_map/ppermute | solution.py:127
  140.7 180.7 %collective-permute-start = (bf16[1024,4096]{1,0:T(8,128)(2,1)}, bf16[1024,4096]{1,0:T(8,128)(2,1)}, u32[]{:S(2)}, u32[]{:S(2)}) collective-permute-start(bf16[1024,4096]{1,0:T(8,128)(2,1)} %all-gather.4.cloned.1.call-done), channel_id=1, source_target_pairs={{0,1},{1,0},{2,3},{3,2},{4,5},{5,4},{6,7},{7,6},{8,9},{9,8},{10,11... | collective-permute-start | bytes 25165832 | tf_op jit(solution)/shard_map/ppermute | solution.py:23
  550.6 85.8 %all-to-all-start = ((bf16[1024,4,2,128]{3,0,2,1:T(8,128)(2,1)}), bf16[1024,4,2,128]{3,0,2,1:T(8,128)(2,1)S(1)}, u32[]{:S(2)}, u32[]{:S(2)}) async-start(bf16[1024,4,2,128]{3,0,2,1:T(8,128)(2,1)} %pad_maximum_fusion.2), calls=%async_computation | async-start | bytes 4194304 | tf_op jit(solution)/shard_map/all_to_all | solution.py:144
  554.2 83.7 %all-gather.8.cloned.1.call-start = ((), (), s32[]{:S(2)}) async-start(), calls=%async_computation.5 | async-start | bytes 2621440 | tf_op jit(solution)/shard_map/all_gather | solution.py:139
  637.9 4.8 copy-start
  689.4 11.9 %copy-start.17 = (bf16[2,512,512]{1,2,0:T(8,128)(2,1)S(1)}, bf16[2,512,512]{1,2,0:T(8,128)(2,1)}, u32[]{:S(2)}) copy-start(bf16[2,512,512]{1,2,0:T(8,128)(2,1)} %get-tuple-element.24) | copy-start | bytes 3145732
  706.7 7.6 slice-start
  710.1 4.2 copy-start.6
  710.1 9.5 %slice-start.2 = ((s8[6291456]{0:T(1024)(128)(4,1)}), s8[4194304]{0:T(1024)(128)(4,1)S(1)}, s32[]{:S(2)}) async-start(s8[6291456]{0:T(1024)(128)(4,1)} %bitcast.394), calls=%async_computation.8 | async-start | bytes 8388608
  714.4 5.3 copy-start.5
  714.4 5.2 copy-start.11
  714.4 5.2 slice-start.3
  714.4 11.1 %slice-start.4 = ((s8[7340032]{0:T(1024)(128)(4,1)}), s8[4194304]{0:T(1024)(128)(4,1)S(1)}, s32[]{:S(2)}) async-start(s8[7340032]{0:T(1024)(128)(4,1)} %bitcast.396), calls=%async_computation.10 | async-start | bytes 8388608
  719.6 5.9 copy-start.4
  719.6 5.9 copy-start.10
  719.6 5.8 slice-start.5
  719.6 12.5 %slice-start.6 = ((s8[8388608]{0:T(1024)(128)(4,1)}), s8[4194304]{0:T(1024)(128)(4,1)S(1)}, s32[]{:S(2)}) async-start(s8[8388608]{0:T(1024)(128)(4,1)} %bitcast.398), calls=%async_computation.12 | async-start | bytes 8388608
  725.5 6.7 copy-start.3
  725.5 6.7 copy-start.9
  725.5 6.6 slice-start.7
  (13 other events, 39.6 us)
Sparse Core Ops, SparseCore 0:
  8.9 97.6 all-gather.3
  140.8 356.8 all-gather.5
  556.7 74.4 all-gather.7
